TPU v7x, 512 devices: a whole 4x4x16 slice. The times are simulated.
512 devices in a mesh: fsdp: 32 (over x_lo, z), tp: 16 (over x_hi, y, core).
Axes of the slice: x: 4 (x_hi: 2, x_lo: 2; x = x_hi * 2 + x_lo), y: 4, z: 16, core: 2. Of those that a mesh axis runs over, the one named last changes fastest.
Arguments:
- activations: bfloat16 [16384, 4096], P(('fsdp', 'tp')), may hold values from -6 to 6
- norm_gain: float32 [4096], replicated, may hold values from 0.5 to 1.5
- proj_weight: bfloat16 [3, 4096, 4096], P(None, 'fsdp', 'tp'), may hold values from -0.09375 to 0.09375
- short_filter: float32 [256, 7], P('tp'), may hold values from -3 to 3
- segment_ids: int32 [32, 512], P('fsdp'), may hold values from 0 to 7, never falling along the last dimension, each value on 1 to 256 neighbouring positions
- needle_pos: int32 [32, 16], P('fsdp'), may hold values from 0 to 511
- readout: float32 [4096], replicated, may hold values from -6 to 6
Outputs:
- mixer_out: bfloat16 [16384, 4096], P(('fsdp', 'tp'))
- needle_score: float32 [32, 16], P('fsdp')
Inputs may be any that keep to these rules, and one draw needn't show every extreme that they name: segment_ids never fall along a slab; each document covers 1 to 256 positions.
All inputs are finite; a program needn't handle non-finite values.
Results may differ from a plain program's by a relative error of at most 0.0068.
Values may be sent and summed in bfloat16 or wider, within the bound.
No kernel may reach another device: no remote copies, remote signals or barrier semaphores. Data moves between devices by JAX's collectives and lax.ppermute only.
A program may use at most 64 MiB of HBM per device.

v0:
```python
import math
import jax
import jax.numpy as jnp
from jax import lax
from jax.sharding import PartitionSpec as P

EPSILON = 1e-06


def short_conv(gated_prod, tap_table, segments):
    length = gated_prod.shape[0]
    filtered = jnp.zeros(gated_prod.shape, jnp.float32)
    for offset in range(tap_table.shape[1]):
        shifted = jnp.pad(gated_prod, ((offset, 0), (0, 0)))[:length]
        earlier = jnp.pad(segments, (offset, 0), constant_values=-1)[:length]
        same_doc = (earlier == segments).astype(jnp.float32)
        filtered = filtered + shifted * same_doc[:, None] * tap_table[:, offset][None, :]
    return filtered


def local(activations, norm_gain, proj_weight, short_filter, segment_ids, needle_pos, readout):
    model_width = activations.shape[1]
    local_rows = activations.shape[0]
    tp_size = lax.axis_size("tp")
    channels = proj_weight.shape[2]
    weights = lax.all_gather(proj_weight, "fsdp", axis=1, tiled=True)
    values = activations.astype(jnp.float32)
    scaled = lax.rsqrt(jnp.mean(values * values, axis=1, keepdims=True) + EPSILON)
    normed = (values * scaled * norm_gain[None, :]).astype(jnp.bfloat16)
    spread = jnp.broadcast_to(normed[None], (tp_size,) + normed.shape)
    slab_rows = lax.all_to_all(spread, "tp", 0, 0, tiled=False).reshape(
        tp_size * local_rows, model_width
    )
    projected = jnp.einsum("sk,ikc->isc", slab_rows, weights, preferred_element_type=jnp.float32)
    gated_prod = projected[1] * projected[2]
    tap_table = jnp.repeat(short_filter, channels // short_filter.shape[0], axis=0)
    filtered = short_conv(gated_prod, tap_table, segment_ids[0])
    mixed_local = (projected[0] * filtered).astype(jnp.bfloat16)
    device_rank = lax.axis_index("tp")
    positions = needle_pos[0]
    slab_len = tp_size * local_rows
    picker = (positions[:, None] == jnp.arange(slab_len, dtype=jnp.int32)[None, :]).astype(
        jnp.bfloat16
    )
    picked = jnp.dot(picker, mixed_local, preferred_element_type=jnp.float32)
    own_readout = lax.dynamic_slice_in_dim(readout, device_rank * channels, channels, 0)
    partial_sum = jnp.sum(picked * own_readout[None, :], axis=1)
    partials = lax.all_to_all(
        jnp.broadcast_to(partial_sum[None], (tp_size,) + partial_sum.shape), "tp", 0, 0, tiled=False
    )
    needle_score = (jnp.sum(partials, axis=0) / math.sqrt(model_width))[None, :]
    blocks = mixed_local.reshape(tp_size, local_rows, channels)
    gathered = lax.all_to_all(blocks, "tp", 0, 0, tiled=False)
    own_rows = jnp.transpose(gathered, (1, 0, 2)).reshape(local_rows, tp_size * channels)
    return (own_rows, needle_score)


def solution(mesh):
    in_specs = (
        P(("fsdp", "tp"), None),
        P(),
        P(None, "fsdp", "tp"),
        P("tp", None),
        P("fsdp", None),
        P("fsdp", None),
        P(),
    )
    out_specs = (P(("fsdp", "tp"), None), P("fsdp", None))
    return jax.shard_map(local, mesh=mesh, in_specs=in_specs, out_specs=out_specs, check_vma=False)
```

profile of v0, /device:TPU:1, one launch (start us, length us, event | category | flops | bytes accessed | tf_op | source)
XLA Modules:
  0.0 202.9 jit_solution(14651823412645313950)
XLA Ops:
  7.2 0.0 all-gather.2.cloned.1.call-start
  7.2 0.7 all-gather.2.cloned.1.call-update
  7.9 1.1 fusion.21
  9.0 1.1 fusion.23
  10.1 2.6 %broadcast_in_dim.6 = bf16[16,32,4096]{2,1,0:T(8,128)(2,1)} broadcast(bf16[32,4096]{1,0:T(8,128)(2,1)S(1)} %fusion.23), dimensions={1,2} | broadcast | bytes 4456448 | tf_op jit(solution)/shard_map/broadcast_in_dim | solution.py:30
  12.7 0.0 copy-start
  12.7 0.0 copy-start.1
  12.7 11.3 %all-to-all-start = ((bf16[16,32,4096]{2,1,0:T(8,128)(2,1)}), bf16[16,32,4096]{2,1,0:T(8,128)(2,1)}, u32[]{:S(2)}, u32[]{:S(2)}) async-start(bf16[16,32,4096]{2,1,0:T(8,128)(2,1)} %broadcast_in_dim.6), calls=%async_computation | async-start | bytes 8388608 | tf_op jit(solution)/shard_map/all_to_all | solution.py:31
  24.0 0.0 copy-done
  24.0 0.1 broadcast_in_dim.7
  24.0 0.1 reshape.58
  24.1 0.8 dynamic_slice.3
  24.9 0.0 copy-done.1
  24.9 0.1 fusion.37
  25.0 98.3 %all-to-all-done = bf16[16,32,4096]{2,1,0:T(8,128)(2,1)} async-done(((bf16[16,32,4096]{2,1,0:T(8,128)(2,1)}), bf16[16,32,4096]{2,1,0:T(8,128)(2,1)}, u32[]{:S(2)}, u32[]{:S(2)}) %all-to-all-start) | async-done | bytes 4194336 | tf_op jit(solution)/shard_map/all_to_all | solution.py:31
  123.3 18.9 %all-gather.2.cloned.1.call-done = bf16[3,4096,256]{2,1,0:T(8,128)(2,1)} async-done(((bf16[3,128,256]{2,1,0:T(8,128)(2,1)}), bf16[3,4096,256]{2,1,0:T(8,128)(2,1)}) %all-gather.2.cloned.1.call-update) | async-done | bytes 6291472 | tf_op jit(solution)/shard_map/all_gather | solution.py:26
  142.2 0.0 copy-start.2
  142.2 7.0 %convolution_bitcast_fusion = f32[3,512,256]{2,1,0:T(8,128)S(1)} fusion(bf16[512,4096,1]{1,0,2:T(8,128)(2,1)} %bitcast.1, bf16[3,4096,256]{2,1,0:T(8,128)(2,1)} %all-gather.2.cloned.1.call-done), kind=kOutput, calls=%fused_computation | convolution fusion | flops 3221225472 | bytes 12058624 | tf_op jit(solution)/shard_map/sk,ikc->isc/dot_general | solution.py:34
  149.2 0.1 fusion.24
  149.3 1.5 fusion.10
  150.8 0.0 copy-done.2
  150.8 1.2 fusion
  152.0 30.6 %all_to_all.16 = f32[16,1,16]{2,1,0:T(1,128)S(1)} all-to-all(f32[16,1,16]{2,1,0:T(1,128)S(1)} %broadcast_in_dim.8), channel_id=1, replica_groups=mesh['fsdp'=32,'tp'=16] {'tp'}, dimensions={0} | all-to-all | bytes 2048 | tf_op jit(solution)/shard_map/all_to_all | solution.py:48
  182.6 4.0 %all-to-all-start.1 = ((bf16[16,32,256]{2,1,0:T(8,128)(2,1)}), bf16[16,32,256]{2,1,0:T(8,128)(2,1)S(1)}, u32[]{:S(2)}, u32[]{:S(2)}) async-start(bf16[16,32,256]{2,1,0:T(8,128)(2,1)} %bitcast.13), calls=%async_computation.1 | async-start | bytes 524288 | tf_op jit(solution)/shard_map/all_to_all | solution.py:53
  186.7 0.5 multiply_bitcast_fusion
  187.2 8.2 %all-to-all-done.1 = bf16[16,32,256]{2,1,0:T(8,128)(2,1)S(1)} async-done(((bf16[16,32,256]{2,1,0:T(8,128)(2,1)}), bf16[16,32,256]{2,1,0:T(8,128)(2,1)S(1)}, u32[]{:S(2)}, u32[]{:S(2)}) %all-to-all-start.1) | async-done | bytes 262176 | tf_op jit(solution)/shard_map/all_to_all | solution.py:53
  195.4 0.7 copy.15
  (4 shorter events, 0.0 us)
Async XLA Ops:
  7.2 135.0 %all-gather.2.cloned.1.call-start = ((), (), s32[]{:S(2)}) async-start(), calls=%async_computation.3 | async-start | bytes 6488064 | tf_op jit(solution)/shard_map/all_gather | solution.py:26
  12.7 11.3 %copy-start = (f32[16,7]{0,1:T(8,128)S(1)}, f32[16,7]{0,1:T(8,128)}, u32[]{:S(2)}) copy-start(f32[16,7]{0,1:T(8,128)} %param.10) | copy-start | bytes 1348
  12.7 12.2 %copy-start.1 = (s32[1,512]{1,0:T(1,128)S(1)}, s32[1,512]{1,0:T(1,128)}, u32[]{:S(2)}) copy-start(s32[1,512]{1,0:T(1,128)} %param.11) | copy-start | bytes 6148
  12.7 110.6 %all-to-all-start = ((bf16[16,32,4096]{2,1,0:T(8,128)(2,1)}), bf16[16,32,4096]{2,1,0:T(8,128)(2,1)}, u32[]{:S(2)}, u32[]{:S(2)}) async-start(bf16[16,32,4096]{2,1,0:T(8,128)(2,1)} %broadcast_in_dim.6), calls=%async_computation | async-start | bytes 8388608 | tf_op jit(solution)/shard_map/all_to_all | solution.py:31
  142.2 8.6 %copy-start.2 = (s32[1,16]{1,0:T(1,128)S(1)}, s32[1,16]{1,0:T(1,128)}, u32[]{:S(2)}) copy-start(s32[1,16]{1,0:T(1,128)} %param.12) | copy-start | bytes 196
  182.6 12.7 %all-to-all-start.1 = ((bf16[16,32,256]{2,1,0:T(8,128)(2,1)}), bf16[16,32,256]{2,1,0:T(8,128)(2,1)S(1)}, u32[]{:S(2)}, u32[]{:S(2)}) async-start(bf16[16,32,256]{2,1,0:T(8,128)(2,1)} %bitcast.13), calls=%async_computation.1 | async-start | bytes 524288 | tf_op jit(solution)/shard_map/all_to_all | solution.py:53
Sparse Core Ops, SparseCore 0:
  10.1 132.0 all-gather.1
where the time goes:
time: 203 us
  waiting for transfers between devices  126 us (62%)
  blocking collectives  30.6 us (15%)
  starting transfers between devices  15.3 us (8%)
  between operations  14.1 us (7%)
  matrix products  8.29 us (4%)
  other arithmetic  4.34 us (2%)
  local copies, waits for them, and re-layouts  4.24 us (2%)
    all_to_all x1, waiting for transfers between devices, local(): lax.all_to_all(spread, 'tp', 0, 0, tiled=False)  98.3 us
    all_to_all x1, blocking collectives, local(): lax.all_to_all(jnp.broadcast_to(partial_sum[None], (tp_size,) + partial_s...  30.6 us
    all_gather x1, waiting for transfers between devices, local(): weights = lax.all_gather(proj_weight, 'fsdp', axis=1, tiled=True)  18.9 us
    all_to_all x1, starting transfers between devices, local(): lax.all_to_all(spread, 'tp', 0, 0, tiled=False)  11.3 us
    all_to_all x1, waiting for transfers between devices, local(): gathered = lax.all_to_all(blocks, 'tp', 0, 0, tiled=False)  8.21 us
    dot_general x1, matrix products, local(): jnp.einsum('sk,ikc->isc', slab_rows, weights, preferred_element_type=jnp....  7.04 us
  transfers between devices with their start and end apart: 3, of which 3 were waited for; matrix products, arithmetic and copies ran while one was open for 3% of the time, Pallas kernels for 0%

commit v1 on v0

--- a/solution.py
+++ b/solution.py
@@ -23,7 +23,9 @@
     local_rows = activations.shape[0]
     tp_size = lax.axis_size("tp")
     channels = proj_weight.shape[2]
-    weights = lax.all_gather(proj_weight, "fsdp", axis=1, tiled=True)
+    weights = jnp.concatenate(
+        lax.all_to_all(jnp.stack([proj_weight] * lax.axis_size("fsdp")), "fsdp", 0, 0), axis=1
+    )
     values = activations.astype(jnp.float32)
     scaled = lax.rsqrt(jnp.mean(values * values, axis=1, keepdims=True) + EPSILON)
     normed = (values * scaled * norm_gain[None, :]).astype(jnp.bfloat16)

time: 203 us -> 409 us (2.01)
  waiting for transfers between devices: 126 us -> 329 us
  starting transfers between devices: 15.3 us -> 29.8 us
  between operations: 14.1 us -> 0.71 us
  blocking collectives: 30.6 us -> 19.9 us
  local copies, waits for them, and re-layouts: 4.24 us -> 14.7 us
    all_to_all x0 -> x1, waiting for transfers between devices: none -> 273 us  [local(): lax.all_to_all(jnp.stack([proj_weight] * lax.axis_size('fsdp')), 'fsdp',...]
    all_to_all x1, waiting for transfers between devices: 98.3 us -> 47.8 us  [local(): lax.all_to_all(spread, 'tp', 0, 0, tiled=False)]
    all_gather x1 -> x0, waiting for transfers between devices: 18.9 us -> none  [local(): weights = lax.all_gather(proj_weight, 'fsdp', axis=1, tiled=True)]
    all_to_all x0 -> x1, starting transfers between devices: none -> 17.2 us  [local(): lax.all_to_all(jnp.stack([proj_weight] * lax.axis_size('fsdp')), 'fsdp',...]
    all_to_all x1, blocking collectives: 30.6 us -> 19.9 us  [local(): lax.all_to_all(jnp.broadcast_to(partial_sum[None], (tp_size,) + partial_s...]
    reshape x0 -> x1, local copies, waits for them, and re-layouts: none -> 6.23 us  [local(): jnp.concatenate(lax.all_to_all(jnp.stack([proj_weight] * lax.axis_size('f...]
    another operation x0 -> x1, local copies, waits for them, and re-layouts: none -> 4.35 us  [local(): jnp.stack([proj_weight] * lax.axis_size('fsdp'))]
  transfers between devices with their start and end apart: 3 -> 3, of which waited for: 3 -> 3; matrix products, arithmetic and copies ran while one was open for 3% -> 2% of each run, Pallas kernels for 0% -> 0%
where the time goes in v1:
time: 409 us; the launch traced here: 405 us
  waiting for transfers between devices  329 us (80%)
  starting transfers between devices  29.8 us (7%)
  blocking collectives  19.9 us (5%)
  local copies, waits for them, and re-layouts  14.7 us (4%)
  matrix products  8.29 us (2%)
    all_to_all x1, waiting for transfers between devices, local(): lax.all_to_all(jnp.stack([proj_weight] * lax.axis_size('fsdp')), 'fsdp',...  273 us
    all_to_all x1, waiting for transfers between devices, local(): lax.all_to_all(spread, 'tp', 0, 0, tiled=False)  47.8 us
    all_to_all x1, blocking collectives, local(): lax.all_to_all(jnp.broadcast_to(partial_sum[None], (tp_size,) + partial_s...  19.9 us
    all_to_all x1, starting transfers between devices, local(): lax.all_to_all(jnp.stack([proj_weight] * lax.axis_size('fsdp')), 'fsdp',...  17.2 us
    all_to_all x1, starting transfers between devices, local(): lax.all_to_all(spread, 'tp', 0, 0, tiled=False)  8.63 us
    all_to_all x1, waiting for transfers between devices, local(): gathered = lax.all_to_all(blocks, 'tp', 0, 0, tiled=False)  8.21 us
  transfers between devices with their start and end apart: 3, of which 3 were waited for; matrix products, arithmetic and copies ran while one was open for 2% of the time, Pallas kernels for 0%

profile of v1, /device:TPU:1, one launch (start us, length us, event | category | flops | bytes accessed | tf_op | source)
XLA Modules:
  0.0 405.3 jit_solution(5948755221245836471)
XLA Ops:
  0.6 4.4 %stack.2 = bf16[32,3,128,256]{3,2,1,0:T(8,128)(2,1)} broadcast(bf16[3,128,256]{2,1,0:T(8,128)(2,1)} %param.9), dimensions={1,2,3} | broadcast | bytes 6488064 | tf_op jit(solution)/shard_map/stack | solution.py:27
  5.0 0.0 copy-start
  5.0 0.0 copy-start.1
  5.0 17.2 %all-to-all-start.1 = ((bf16[32,3,128,256]{3,2,1,0:T(8,128)(2,1)}), bf16[32,3,128,256]{3,2,1,0:T(8,128)(2,1)}, u32[]{:S(2)}, u32[]{:S(2)}) async-start(bf16[32,3,128,256]{3,2,1,0:T(8,128)(2,1)} %stack.2), calls=%async_computation.1 | async-start | bytes 12582912 | tf_op jit(solution)/shard_map/all_to_all | solution.py:27
  22.2 0.0 copy-done
  22.2 0.2 fusion.21
  22.4 0.0 copy-done.1
  22.4 0.1 fusion.23
  22.5 273.4 %all-to-all-done.1 = bf16[32,3,128,256]{3,2,1,0:T(8,128)(2,1)} async-done(((bf16[32,3,128,256]{3,2,1,0:T(8,128)(2,1)}), bf16[32,3,128,256]{3,2,1,0:T(8,128)(2,1)}, u32[]{:S(2)}, u32[]{:S(2)}) %all-to-all-start.1) | async-done | bytes 6291488 | tf_op jit(solution)/shard_map/all_to_all | solution.py:27
  295.9 2.4 broadcast_in_dim.6
  298.3 0.0 copy-start.2
  298.3 0.0 copy-start.3
  298.3 8.6 %all-to-all-start = ((bf16[16,32,4096]{2,1,0:T(8,128)(2,1)}), bf16[16,32,4096]{2,1,0:T(8,128)(2,1)}, u32[]{:S(2)}, u32[]{:S(2)}) async-start(bf16[16,32,4096]{2,1,0:T(8,128)(2,1)} %broadcast_in_dim.6), calls=%async_computation | async-start | bytes 8388608 | tf_op jit(solution)/shard_map/all_to_all | solution.py:33
  307.0 0.0 copy-done.2
  307.0 0.1 broadcast_in_dim.7
  307.0 0.1 reshape.68
  307.1 0.8 dynamic_slice.3
  307.9 0.0 copy-done.3
  307.9 0.1 fusion.37
  308.0 6.2 %copy.16 = bf16[3,32,128,256]{3,2,1,0:T(8,128)(2,1)} copy(bf16[3,32,128,256]{3,2,0,1:T(8,128)(2,1)} %bitcast.2) | data formatting | bytes 12582912 | tf_op jit(solution)/shard_map/reshape | solution.py:26
  314.2 47.8 %all-to-all-done = bf16[16,32,4096]{2,1,0:T(8,128)(2,1)} async-done(((bf16[16,32,4096]{2,1,0:T(8,128)(2,1)}), bf16[16,32,4096]{2,1,0:T(8,128)(2,1)}, u32[]{:S(2)}, u32[]{:S(2)}) %all-to-all-start) | async-done | bytes 4194336 | tf_op jit(solution)/shard_map/all_to_all | solution.py:33
  362.0 0.0 copy-start.4
  362.0 7.0 %convolution_bitcast_fusion = f32[3,512,256]{2,1,0:T(8,128)S(1)} fusion(bf16[512,4096,1]{1,0,2:T(8,128)(2,1)} %bitcast.1, bf16[3,4096,256]{2,1,0:T(8,128)(2,1)} %bitcast.34), kind=kOutput, calls=%fused_computation | convolution fusion | flops 3221225472 | bytes 12058624 | tf_op jit(solution)/shard_map/sk,ikc->isc/dot_general | solution.py:36
  369.1 0.1 fusion.24
  369.2 1.5 fusion.10
  370.6 0.0 copy-done.4
  370.6 1.2 fusion
  371.9 19.9 %all_to_all.21 = f32[16,1,16]{2,1,0:T(1,128)S(1)} all-to-all(f32[16,1,16]{2,1,0:T(1,128)S(1)} %broadcast_in_dim.8), channel_id=1, replica_groups=mesh['fsdp'=32,'tp'=16] {'tp'}, dimensions={0} | all-to-all | bytes 2048 | tf_op jit(solution)/shard_map/all_to_all | solution.py:50
  391.8 4.0 all-to-all-start.2
  395.8 0.5 multiply_bitcast_fusion
  396.4 8.2 %all-to-all-done.2 = bf16[16,32,256]{2,1,0:T(8,128)(2,1)S(1)} async-done(((bf16[16,32,256]{2,1,0:T(8,128)(2,1)}), bf16[16,32,256]{2,1,0:T(8,128)(2,1)S(1)}, u32[]{:S(2)}, u32[]{:S(2)}) %all-to-all-start.2) | async-done | bytes 262176 | tf_op jit(solution)/shard_map/all_to_all | solution.py:55
  404.6 0.7 copy.19
  (4 shorter events, 0.0 us)
Async XLA Ops:
  5.0 17.2 %copy-start = (bf16[32,4096]{1,0:T(8,128)(2,1)S(1)}, bf16[32,4096]{1,0:T(8,128)(2,1)}, u32[]{:S(2)}) copy-start(bf16[32,4096]{1,0:T(8,128)(2,1)} %param.7) | copy-start | bytes 786436
  5.0 17.4 %copy-start.1 = (f32[4096]{0:T(1024)S(1)}, f32[4096]{0:T(1024)}, u32[]{:S(2)}) copy-start(f32[4096]{0:T(1024)} %param.8) | copy-start | bytes 49156
  5.0 290.9 %all-to-all-start.1 = ((bf16[32,3,128,256]{3,2,1,0:T(8,128)(2,1)}), bf16[32,3,128,256]{3,2,1,0:T(8,128)(2,1)}, u32[]{:S(2)}, u32[]{:S(2)}) async-start(bf16[32,3,128,256]{3,2,1,0:T(8,128)(2,1)} %stack.2), calls=%async_computation.1 | async-start | bytes 12582912 | tf_op jit(solution)/shard_map/all_to_all | solution.py:27
  298.3 8.6 %copy-start.2 = (f32[16,7]{0,1:T(8,128)S(1)}, f32[16,7]{0,1:T(8,128)}, u32[]{:S(2)}) copy-start(f32[16,7]{0,1:T(8,128)} %param.10) | copy-start | bytes 1348
  298.3 9.6 %copy-start.3 = (s32[1,512]{1,0:T(1,128)S(1)}, s32[1,512]{1,0:T(1,128)}, u32[]{:S(2)}) copy-start(s32[1,512]{1,0:T(1,128)} %param.11) | copy-start | bytes 6148
  298.3 63.7 %all-to-all-start = ((bf16[16,32,4096]{2,1,0:T(8,128)(2,1)}), bf16[16,32,4096]{2,1,0:T(8,128)(2,1)}, u32[]{:S(2)}, u32[]{:S(2)}) async-start(bf16[16,32,4096]{2,1,0:T(8,128)(2,1)} %broadcast_in_dim.6), calls=%async_computation | async-start | bytes 8388608 | tf_op jit(solution)/shard_map/all_to_all | solution.py:33
  362.0 8.6 %copy-start.4 = (s32[1,16]{1,0:T(1,128)S(1)}, s32[1,16]{1,0:T(1,128)}, u32[]{:S(2)}) copy-start(s32[1,16]{1,0:T(1,128)} %param.12) | copy-start | bytes 196
  391.8 12.7 %all-to-all-start.2 = ((bf16[16,32,256]{2,1,0:T(8,128)(2,1)}), bf16[16,32,256]{2,1,0:T(8,128)(2,1)S(1)}, u32[]{:S(2)}, u32[]{:S(2)}) async-start(bf16[16,32,256]{2,1,0:T(8,128)(2,1)} %bitcast.15), calls=%async_computation.2 | async-start | bytes 524288 | tf_op jit(solution)/shard_map/all_to_all | solution.py:55
